TPU v7x, 128 devices: a whole 4x4x4 slice. The times are simulated.
128 devices in a mesh: sec: 2 (over core), tile: 64 (over y, x, z).
Axes of the slice: x: 4, y: 4, z: 4, core: 2. Of those that a mesh axis runs over, the one named last changes fastest.
Arguments:
- land_wind: float32 [16384, 128], P(('sec', 'tile')), may hold values from 0.15 to 0.9
- land_moist: float32 [16384, 128], P(('sec', 'tile')), may hold values from 0 to 0.3
- texture: int32 [16384, 128], P(('sec', 'tile')), may hold values from 0 to 3
- land_index: int32 [16384, 128], P(('sec', 'tile')), may hold values from 0 to 32767
- erod_map: float32 [4194304], P(('sec', 'tile')), may hold values from 0.2 to 1
- mass_frac: float32 [4, 12], replicated, may hold values from 0.02 to 0.3
- blast_table: float32 [4, 8, 12], replicated, may hold values from 0.05 to 1
- dest_tile: int32 [16384, 1], P(('sec', 'tile')), may hold values from 0 to 127; in each aligned block of 128 rows (0 to 127, 128 to 255, ...) at most 2 rows name the same one
- regrid_w: bfloat16 [16384, 128, 256], P(('sec', 'tile')), may hold values from 0 to 0.25, as said below
- atm_state: float32 [3, 16, 32768], P(None, None, ('sec', 'tile')), may hold values from -5 to 5
- dust_mix: float32 [8, 16, 32768], P(None, None, ('sec', 'tile')), may hold values from 0 to 1
- mixing: float32 [15, 32768], P(None, ('sec', 'tile')), may hold values from 0.1 to 10
- settle: float32 [8], replicated, may hold values from 0.05 to 0.5
Outputs:
- land_fields: float32 [2, 16384, 128], P(None, ('sec', 'tile'))
- dust_out: float32 [8, 16, 32768], P(None, None, ('sec', 'tile'))
Inputs may be any that keep to these rules, and one draw needn't show every extreme that they name: `land_index`: each land cell's index points into its own device's 32768 cells of erod_map. `dest_tile`: among the 128 blocks of one device at most 2 name the same tile, a bound that some block reaches. `regrid_w`: each land cell has 1 to 4 positive weights, of 0.05 or more, on adjacent columns of its tile, and 0 elsewhere.
All inputs are finite; a program needn't handle non-finite values.
Results may differ from a plain program's by a relative error of at most 0.0023.
Values may be sent and summed in bfloat16 or wider, within the bound.
No kernel may reach another device: no remote copies, remote signals or barrier semaphores. Data moves between devices by JAX's collectives and lax.ppermute only.
A program may use at most 64 MiB of HBM per device.

v0:
```python
import jax
import jax.numpy as jnp
from jax import lax
from jax.sharding import PartitionSpec as P


def threshold_table(count):
    diameter = 4e-05 * jnp.power(jnp.float32(1.35), jnp.arange(count).astype(jnp.float32))
    return jnp.sqrt(0.0123 * (2160.0 * 9.81 * diameter + 0.0003 / (1.227 * diameter)))


def emit(wind_rows, moist_rows, texture_rows, erodible, mass_frac, blast_table, base_thresh):
    high = lax.Precision.HIGHEST
    thresh = base_thresh[:, None, None] * jnp.sqrt(1.0 + 12.1 * moist_rows)[None]
    classes = jnp.arange(mass_frac.shape[0])
    onehot = (texture_rows[None] == classes[:, None, None]).astype(jnp.float32)
    fraction = jnp.einsum("tb,tnl->bnl", mass_frac, onehot, precision=high)
    speed = wind_rows[None]
    salt = (
        40.0
        * fraction
        * erodible[None]
        * (speed + thresh)
        * jnp.maximum(speed * speed - thresh * thresh, 0.0)
    )
    blasted = jnp.einsum("tkb,bnl->tknl", blast_table, salt, precision=high)
    emission = jnp.sum(blasted * onehot[:, None], axis=0)
    return jnp.transpose(emission, (1, 0, 2)).astype(jnp.bfloat16)


def solve(right_side, coupling, sinking):
    levels = right_side.shape[1]
    sink_col = sinking[:, None]
    zero_row = jnp.zeros_like(coupling[0])
    ratios = []
    partial_value = []
    ratio_prev = None
    part_prev = None
    for level in range(levels):
        lower_c = coupling[level - 1] if level > 0 else zero_row
        upper_c = coupling[level] if level < levels - 1 else zero_row
        diagonal = 1.0 + lower_c[None] + upper_c[None] + sink_col
        if level == 0:
            pivot = diagonal
            part_now = right_side[:, level] / pivot
        else:
            pivot = diagonal + lower_c[None] * ratio_prev
            part_now = (right_side[:, level] + lower_c[None] * part_prev) / pivot
        if level < levels - 1:
            ratio_now = -(upper_c[None] + sink_col) / pivot
        else:
            ratio_now = jnp.zeros_like(pivot)
        ratios.append(ratio_now)
        partial_value.append(part_now)
        ratio_prev = ratio_now
        part_prev = part_now
    result = [None] * levels
    result[levels - 1] = partial_value[levels - 1]
    for level in range(levels - 2, -1, -1):
        result[level] = partial_value[level] - ratios[level] * result[level + 1]
    return jnp.stack(result, axis=1)


def on_device(
    land_wind,
    land_moist,
    texture,
    land_index,
    erod_map,
    mass_frac,
    blast_table,
    dest_tile,
    regrid_w,
    atm_state,
    dust_mix,
    mixing,
    settle,
):
    high = lax.Precision.HIGHEST
    nblocks, ncells = land_wind.shape
    columns = atm_state.shape[2]
    nbins = blast_table.shape[1]
    devices = lax.axis_size(("sec", "tile"))
    state = solve(atm_state, mixing, jnp.zeros((3,), jnp.float32))
    speed = jnp.sqrt(state[0, 0] ** 2 + state[1, 0] ** 2 + 0.25)
    surface = jnp.stack([speed, state[2, 0]]).astype(jnp.bfloat16).reshape(1, 2 * columns)
    gathered = lax.all_gather(surface, ("sec", "tile"), axis=0, tiled=True)
    base_thresh = threshold_table(mass_frac.shape[1])
    erodible = erod_map[land_index]
    emission = emit(land_wind, land_moist, texture, erodible, mass_frac, blast_table, base_thresh)
    partial_flux = jnp.einsum(
        "gkl,gla->gka", emission, regrid_w, preferred_element_type=jnp.float32
    )
    flat_flux = partial_flux.reshape(nblocks, nbins * columns)
    targets = dest_tile[:, 0]
    onehot = (targets[:, None] == jnp.arange(devices)[None, :]).astype(jnp.float32)
    capacity = max(2, 2 * nblocks // devices)
    before = jnp.cumsum(onehot, axis=0) - onehot
    ranking = jnp.sum(before * onehot, axis=1).astype(jnp.int32)
    slot_of = targets * capacity + ranking
    placing = (jnp.arange(devices * capacity)[:, None] == slot_of[None, :]).astype(jnp.float32)
    outgoing = jnp.dot(placing, flat_flux, precision=high).reshape(
        devices, capacity * nbins * columns
    )
    incoming = lax.all_to_all(
        outgoing.astype(jnp.bfloat16), ("sec", "tile"), split_axis=0, concat_axis=0, tiled=True
    ).astype(outgoing.dtype)
    flux = jnp.sum(incoming.reshape(devices * capacity, nbins, columns), axis=0)
    flux = flux * (float(columns) / float(ncells * nblocks))
    loaded = dust_mix.at[:, 0, :].add(flux)
    dust_out = solve(loaded, mixing, settle)
    picked = jnp.dot(onehot.astype(jnp.bfloat16), gathered, preferred_element_type=jnp.float32)
    picked = picked.astype(jnp.bfloat16).reshape(nblocks, 2, columns)
    numer = jnp.einsum("gla,gka->kgl", regrid_w, picked, preferred_element_type=jnp.float32)
    denom = jnp.sum(regrid_w, axis=2, dtype=jnp.float32)
    land_fields = jnp.stack([numer[0] / denom, 0.5 * land_moist + 0.5 * numer[1] / denom])
    return (land_fields, dust_out)


def solution(mesh):
    in_specs = (
        P(("sec", "tile"), None),
        P(("sec", "tile"), None),
        P(("sec", "tile"), None),
        P(("sec", "tile"), None),
        P(("sec", "tile")),
        P(),
        P(),
        P(("sec", "tile"), None),
        P(("sec", "tile"), None, None),
        P(None, None, ("sec", "tile")),
        P(None, None, ("sec", "tile")),
        P(None, ("sec", "tile")),
        P(),
    )
    out_specs = (P(None, ("sec", "tile"), None), P(None, None, ("sec", "tile")))
    return jax.shard_map(
        on_device, mesh=mesh, in_specs=in_specs, out_specs=out_specs, check_vma=False
    )
```

profile of v0, /device:TPU:1, one launch (start us, length us, event | category | flops | bytes accessed | tf_op | source)
XLA Modules:
  0.0 481.6 jit_solution(7172732893140782613)
XLA Ops:
  0.6 1.0 fusion.78
  1.7 1.0 broadcast_add_fusion.1
  2.7 0.9 fusion.79
  3.6 1.2 fusion.77
  5.4 321.0 %all-gather = bf16[128,1,512]{2,1,0:T(2,128)(2,1)S(1)} all-gather(bf16[1,1,512]{2,1,0:T(2,128)(2,1)S(1)} %reshape.27177), channel_id=1, replica_groups=mesh['sec'=2,'tile'=64] {'sec','tile'}, dimensions={0}, use_global_device_ids=true | all-gather | bytes 132096 | tf_op jit(solution)/shard_map/all_gather | solution.py:87
  326.4 0.7 fusion.17
  327.1 0.9 convolution_convert_fusion.1
  328.1 5.8 %convert_reduce_fusion = f32[128,128]{1,0:T(8,128)S(1)} fusion(bf16[128,128,256]{2,1,0:T(8,128)(2,1)} %param.23), kind=kLoop, calls=%fused_computation.1 | loop fusion | flops 8372224 | bytes 8454144 | tf_op jit(solution)/shard_map/reduce_sum | solution.py:115
  333.9 2.3 convolution_bitcast_fusion
  336.3 90.5 %gather_fusion = f32[16384]{0:T(1024)S(1)} fusion(f32[32768]{0:T(1024)S(1)} %copy-done, s32[16384]{0:T(1024)S(1)} %fusion.15), kind=kCustom, calls=%fused_computation | custom fusion | bytes 196608 | tf_op jit(solution)/shard_map/gather | solution.py:89
  427.1 0.8 fusion.4
  427.9 1.9 fusion
  429.8 4.6 fusion.7
  435.2 1.0 convolution_convert_fusion
  436.2 1.9 convert_element_type.86
  438.7 7.0 %reduce.4 = bf16[128,4096]{1,0:T(8,128)(2,1)S(1)} reduce(bf16[128,1,4096]{2,1,0:T(2,128)(2,1)S(1)} %convert_element_type.86, bf16[]{:T(256)} %broadcast.18933), dimensions={1}, to_apply=%convert_element_type.86.reduce_sub_computation | reduce | bytes 2097154 | tf_op jit(solution)/shard_map/convert_element_type | solution.py:106
  445.7 1.6 reshape.27184
  447.3 3.8 all-to-all-start
  451.1 0.7 pad_maximum_fusion
  451.9 16.8 %all-to-all-done = bf16[128,2,2048]{2,1,0:T(2,128)(2,1)S(1)} async-done(((bf16[128,2,2048]{2,1,0:T(2,128)(2,1)}), bf16[128,2,2048]{2,1,0:T(2,128)(2,1)S(1)}, u32[]{:S(2)}, u32[]{:S(2)}) %all-to-all-start) | async-done | bytes 1048608 | tf_op jit(solution)/shard_map/all_to_all | solution.py:105
  468.7 1.0 reshape.27185
  469.7 7.5 %convert_reduce_fusion.1 = f32[128,4096]{1,0:T(8,128)} fusion(bf16[128,1,4096]{2,1,0:T(2,128)(2,1)S(1)} %reshape.27185), kind=kLoop, calls=%fused_computation.5 | loop fusion | flops 524288 | bytes 3145728 | tf_op jit(solution)/shard_map/convert_element_type | solution.py:107
  477.2 1.7 reshape.27164
  480.9 0.7 copy.100
  (105 shorter events, 4.0 us)
Async XLA Ops:
  0.6 335.6 %copy-start = (f32[32768]{0:T(1024)S(1)}, f32[32768]{0:T(1024)}, u32[]{:S(2)}) copy-start(f32[32768]{0:T(1024)} %param.19) | copy-start | bytes 393220
  1.6 3.4 copy-start.14
  1.6 3.4 copy-start.16
  1.6 3.4 copy-start.18
  1.7 3.5 copy-start.24
  2.7 2.2 copy-start.8
  2.7 2.4 copy-start.10
  2.7 2.4 copy-start.12
  2.7 2.4 copy-start.20
  2.7 2.4 copy-start.22
  2.7 2.5 copy-start.27
  2.7 2.6 copy-start.29
  328.0 5.8 %copy-start.1 = (bf16[128,128,256]{2,1,0:T(8,128)(2,1)S(1)}, bf16[128,128,256]{2,1,0:T(8,128)(2,1)}, u32[]{:S(2)}) copy-start(bf16[128,128,256]{2,1,0:T(8,128)(2,1)} %param.23) | copy-start | bytes 25165828
  333.8 2.4 copy-start.6
  336.3 90.6 %copy-start.2 = (f32[128,128]{1,0:T(8,128)S(1)}, f32[128,128]{1,0:T(8,128)}, u32[]{:S(2)}) copy-start(f32[128,128]{1,0:T(8,128)} %param.15) | copy-start | bytes 196612
  336.3 90.6 %copy-start.5 = (s32[128,128]{1,0:T(8,128)S(1)}, s32[128,128]{1,0:T(8,128)}, u32[]{:S(2)}) copy-start(s32[128,128]{1,0:T(8,128)} %param.17) | copy-start | bytes 196612
  336.3 90.7 %copy-start.4 = (f32[128,128]{1,0:T(8,128)S(1)}, f32[128,128]{1,0:T(8,128)}, u32[]{:S(2)}) copy-start(f32[128,128]{1,0:T(8,128)} %param.16) | copy-start | bytes 196612
  336.3 90.7 %copy-start.32 = (f32[4,12]{1,0:T(4,128)S(1)}, f32[4,12]{1,0:T(4,128)}, u32[]{:S(2)}) copy-start(f32[4,12]{1,0:T(4,128)} %param.20) | copy-start | bytes 580
  426.9 1.0 copy-start.26
  445.7 6.1 %copy-start.3 = (f32[8,16,256]{2,1,0:T(8,128)S(1)}, f32[8,16,256]{2,1,0:T(8,128)}, u32[]{:S(2)}) copy-start(f32[8,16,256]{2,1,0:T(8,128)} %param.25) | copy-start | bytes 393220
  447.3 21.3 %all-to-all-start = ((bf16[128,2,2048]{2,1,0:T(2,128)(2,1)}), bf16[128,2,2048]{2,1,0:T(2,128)(2,1)S(1)}, u32[]{:S(2)}, u32[]{:S(2)}) async-start(bf16[128,2,2048]{2,1,0:T(2,128)(2,1)} %reshape.27184), calls=%async_computation | async-start | bytes 2097152 | tf_op jit(solution)/shard_map/all_to_all | solution.py:105
  479.0 0.8 copy-start.15
  479.0 0.8 copy-start.17
  479.0 0.8 copy-start.19
  (10 other events, 6.7 us)
where the time goes:
time: 482 us
  blocking collectives  321 us (67%)
  local copies, waits for them, and re-layouts  101 us (21%)
  other arithmetic  26 us (5%)
  waiting for transfers between devices  16.8 us (3%)
  matrix products  11.4 us (2%)
    all_gather x1, blocking collectives, on_device(): gathered = lax.all_gather(surface, ('sec', 'tile'), axis=0, tiled=True)  321 us
    gather x1, local copies, waits for them, and re-layouts, on_device(): erodible = erod_map[land_index]  90.5 us
    all_to_all x1, waiting for transfers between devices, on_device(): lax.all_to_all(outgoing.astype(jnp.bfloat16), ('sec', 'tile'), split_axis...  16.8 us
  transfers between devices with their start and end apart: 1, of which 1 were waited for; matrix products, arithmetic and copies ran while one was open for 0% of the time, Pallas kernels for 0%

commit v1 on v0

--- a/solution.py
+++ b/solution.py
@@ -84,7 +84,8 @@
     state = solve(atm_state, mixing, jnp.zeros((3,), jnp.float32))
     speed = jnp.sqrt(state[0, 0] ** 2 + state[1, 0] ** 2 + 0.25)
     surface = jnp.stack([speed, state[2, 0]]).astype(jnp.bfloat16).reshape(1, 2 * columns)
-    gathered = lax.all_gather(surface, ("sec", "tile"), axis=0, tiled=True)
+    spread = jnp.broadcast_to(surface, (devices, 2 * columns))
+    gathered = lax.all_to_all(spread, ("sec", "tile"), split_axis=0, concat_axis=0, tiled=True)
     base_thresh = threshold_table(mass_frac.shape[1])
     erodible = erod_map[land_index]
     emission = emit(land_wind, land_moist, texture, erodible, mass_frac, blast_table, base_thresh)

time: 482 us -> 184 us (0.38)
  blocking collectives: 321 us -> 0 us
  starting transfers between devices: 3.78 us -> 21.3 us
    all_gather x1 -> x0, blocking collectives: 321 us -> none  [on_device(): gathered = lax.all_gather(surface, ('sec', 'tile'), axis=0, tiled=True)]
    all_to_all x0 -> x1, starting transfers between devices: none -> 11.5 us  [on_device(): lax.all_to_all(spread, ('sec', 'tile'), split_axis=0, concat_axis=0, tile...]
    all_to_all x1, starting transfers between devices: 3.78 us -> 9.77 us  [on_device(): lax.all_to_all(outgoing.astype(jnp.bfloat16), ('sec', 'tile'), split_axis...]
  transfers between devices with their start and end apart: 1 -> 2, of which waited for: 1 -> 1; matrix products, arithmetic and copies ran while one was open for 0% -> 54% of each run, Pallas kernels for 0% -> 0%
where the time goes in v1:
time: 184 us; the launch traced here: 183 us
  local copies, waits for them, and re-layouts  103 us (56%)
  other arithmetic  26.6 us (14%)
  starting transfers between devices  21.3 us (12%)
  waiting for transfers between devices  16.3 us (9%)
  matrix products  14.1 us (8%)
  between operations  2.04 us (1%)
    gather x1, local copies, waits for them, and re-layouts, on_device(): erodible = erod_map[land_index]  90.5 us
    all_to_all x1, waiting for transfers between devices, on_device(): lax.all_to_all(outgoing.astype(jnp.bfloat16), ('sec', 'tile'), split_axis...  16.2 us
    all_to_all x1, starting transfers between devices, on_device(): lax.all_to_all(spread, ('sec', 'tile'), split_axis=0, concat_axis=0, tile...  11.5 us
    all_to_all x1, starting transfers between devices, on_device(): lax.all_to_all(outgoing.astype(jnp.bfloat16), ('sec', 'tile'), split_axis...  9.77 us
    convert_element_type x1, other arithmetic, on_device(): incoming = lax.all_to_all(outgoing.astype(jnp.bfloat16), ('sec', 'tile'),...  7.46 us
    convert_element_type x1, other arithmetic, on_device(): outgoing.astype(jnp.bfloat16)  7.03 us
    dot_general x1, matrix products, on_device(): jnp.einsum('gla,gka->kgl', regrid_w, picked, preferred_element_type=jnp.f...  5.66 us
    reduce_sum x1, other arithmetic, on_device(): denom = jnp.sum(regrid_w, axis=2, dtype=jnp.float32)  5.65 us
  transfers between devices with their start and end apart: 2, of which 1 were waited for; matrix products, arithmetic and copies ran while one was open for 54% of the time, Pallas kernels for 0%

profile of v1, /device:TPU:1, one launch (start us, length us, event | category | flops | bytes accessed | tf_op | source)
XLA Modules:
  0.0 183.0 jit_solution(8447883691844025357)
XLA Ops:
  0.6 1.0 fusion.78
  1.7 1.0 broadcast_add_fusion.1
  2.9 0.9 fusion.79
  3.8 1.2 fusion.77
  6.3 1.4 reduce.4
  7.7 0.7 reshape.27182
  8.4 11.5 %all-to-all-start = ((bf16[128,2,256]{2,1,0:T(2,128)(2,1)}), bf16[128,2,256]{2,1,0:T(2,128)(2,1)S(1)}, u32[]{:S(2)}, u32[]{:S(2)}) async-start(bf16[128,2,256]{2,1,0:T(2,128)(2,1)} %reshape.27182), calls=%async_computation | async-start | bytes 262144 | tf_op jit(solution)/shard_map/all_to_all | solution.py:88
  19.9 5.6 %convert_reduce_fusion = f32[128,128]{1,0:T(8,128)S(1)} fusion(bf16[128,128,256]{2,1,0:T(8,128)(2,1)} %param.23), kind=kLoop, calls=%fused_computation.1 | loop fusion | flops 8372224 | bytes 8454144 | tf_op jit(solution)/shard_map/reduce_sum | solution.py:116
  25.7 90.5 %gather_fusion = f32[16384]{0:T(1024)S(1)} fusion(f32[32768]{0:T(1024)S(1)} %copy-done, s32[16384]{0:T(1024)S(1)} %fusion.15), kind=kCustom, calls=%fused_computation | custom fusion | bytes 196608 | tf_op jit(solution)/shard_map/gather | solution.py:90
  117.3 5.7 %convolution_bitcast_fusion = f32[2,128,128]{2,0,1:T(2,128)S(1)} fusion(bf16[128,2,256]{2,1,0:T(2,128)(2,1)S(1)} %reshape.27163, bf16[128,128,256]{2,1,0:T(8,128)(2,1)} %param.23), kind=kOutput, calls=%fused_computation.14 | convolution fusion | flops 16777216 | bytes 8650752 | tf_op jit(solution)/shard_map/gla,gka->kgl/dot_general | solution.py:115
  123.1 0.8 fusion.4
  124.0 1.8 fusion
  125.8 4.6 %fusion.7 = f32[128,8,256]{2,1,0:T(8,128)S(1)} fusion(bf16[128,128,256]{2,1,0:T(8,128)(2,1)} %param.23, bf16[8,128,128]{2,0,1:T(8,128)(2,1)S(1)} %fusion), kind=kOutput, calls=%fused_computation.17 | convolution fusion | flops 67108864 | bytes 9699328 | tf_op jit(solution)/shard_map/gkl,gla->gka/dot_general | solution.py:92
  130.7 1.0 convolution_convert_fusion
  131.7 1.9 %convert_element_type.83 = bf16[128,1,4096]{2,1,0:T(2,128)(2,1)S(1)} reshape(bf16[256,2048]{1,0:T(8,128)(2,1)S(1)} %convolution_convert_fusion) | data formatting | bytes 2097152 | tf_op jit(solution)/shard_map/convert_element_type | solution.py:107
  133.6 7.0 %reduce.5 = bf16[128,4096]{1,0:T(8,128)(2,1)S(1)} reduce(bf16[128,1,4096]{2,1,0:T(2,128)(2,1)S(1)} %convert_element_type.83, bf16[]{:T(256)} %broadcast.18937), dimensions={1}, to_apply=%convert_element_type.83.reduce_sub_computation | reduce | bytes 2097154 | tf_op jit(solution)/shard_map/convert_element_type | solution.py:107
  140.7 1.6 reshape.27184
  142.3 9.8 %all-to-all-start.1 = ((bf16[128,2,2048]{2,1,0:T(2,128)(2,1)}), bf16[128,2,2048]{2,1,0:T(2,128)(2,1)S(1)}, u32[]{:S(2)}, u32[]{:S(2)}) async-start(bf16[128,2,2048]{2,1,0:T(2,128)(2,1)} %reshape.27184), calls=%async_computation.1 | async-start | bytes 2097152 | tf_op jit(solution)/shard_map/all_to_all | solution.py:106
  152.1 0.7 fusion.75
  153.4 16.2 %all-to-all-done.1 = bf16[128,2,2048]{2,1,0:T(2,128)(2,1)S(1)} async-done(((bf16[128,2,2048]{2,1,0:T(2,128)(2,1)}), bf16[128,2,2048]{2,1,0:T(2,128)(2,1)S(1)}, u32[]{:S(2)}, u32[]{:S(2)}) %all-to-all-start.1) | async-done | bytes 1048608 | tf_op jit(solution)/shard_map/all_to_all | solution.py:106
  169.7 1.0 reshape.27185
  170.8 7.5 %convert_reduce_fusion.1 = f32[128,4096]{1,0:T(8,128)} fusion(bf16[128,1,4096]{2,1,0:T(2,128)(2,1)S(1)} %reshape.27185), kind=kLoop, calls=%fused_computation.5 | loop fusion | flops 524288 | bytes 3145728 | tf_op jit(solution)/shard_map/convert_element_type | solution.py:108
  178.2 1.7 reshape.27165
  182.3 0.7 copy.99
  (194 shorter events, 5.0 us)
Async XLA Ops:
  0.6 25.0 %copy-start = (f32[32768]{0:T(1024)S(1)}, f32[32768]{0:T(1024)}, u32[]{:S(2)}) copy-start(f32[32768]{0:T(1024)} %param.19) | copy-start | bytes 393220
  1.6 3.8 %copy-start.17 = (f32[1,256]{1,0:T(1,128)}, f32[1,256]{1,0:T(1,128)S(1)}, u32[]{:S(2)}) copy-start(f32[1,256]{1,0:T(1,128)S(1)} %get-tuple-element.116) | copy-start | bytes 3076
  1.6 3.8 %copy-start.19 = (f32[1,256]{1,0:T(1,128)}, f32[1,256]{1,0:T(1,128)S(1)}, u32[]{:S(2)}) copy-start(f32[1,256]{1,0:T(1,128)S(1)} %get-tuple-element.117) | copy-start | bytes 3076
  1.6 3.8 %copy-start.27 = (f32[1,256]{1,0:T(1,128)}, f32[1,256]{1,0:T(1,128)S(1)}, u32[]{:S(2)}) copy-start(f32[1,256]{1,0:T(1,128)S(1)} %get-tuple-element.110) | copy-start | bytes 3076
  1.7 3.8 %copy-start.38 = (f32[1,256]{1,0:T(1,128)}, f32[1,256]{1,0:T(1,128)S(1)}, u32[]{:S(2)}) copy-start(f32[1,256]{1,0:T(1,128)S(1)} %get-tuple-element.111) | copy-start | bytes 3076
  1.7 3.8 %copy-start.40 = (f32[1,256]{1,0:T(1,128)}, f32[1,256]{1,0:T(1,128)S(1)}, u32[]{:S(2)}) copy-start(f32[1,256]{1,0:T(1,128)S(1)} %get-tuple-element.112) | copy-start | bytes 3076
  1.7 3.8 %copy-start.42 = (f32[1,256]{1,0:T(1,128)}, f32[1,256]{1,0:T(1,128)S(1)}, u32[]{:S(2)}) copy-start(f32[1,256]{1,0:T(1,128)S(1)} %get-tuple-element.122) | copy-start | bytes 3076
  1.7 3.8 %copy-start.56 = (f32[1,256]{1,0:T(1,128)}, f32[1,256]{1,0:T(1,128)S(1)}, u32[]{:S(2)}) copy-start(f32[1,256]{1,0:T(1,128)S(1)} %get-tuple-element.113) | copy-start | bytes 3076
  1.7 3.8 %copy-start.58 = (f32[1,256]{1,0:T(1,128)}, f32[1,256]{1,0:T(1,128)S(1)}, u32[]{:S(2)}) copy-start(f32[1,256]{1,0:T(1,128)S(1)} %get-tuple-element.114) | copy-start | bytes 3076
  1.7 3.8 %copy-start.60 = (f32[1,256]{1,0:T(1,128)}, f32[1,256]{1,0:T(1,128)S(1)}, u32[]{:S(2)}) copy-start(f32[1,256]{1,0:T(1,128)S(1)} %get-tuple-element.115) | copy-start | bytes 3076
  1.7 3.8 %copy-start.66 = (f32[1,256]{1,0:T(1,128)}, f32[1,256]{1,0:T(1,128)S(1)}, u32[]{:S(2)}) copy-start(f32[1,256]{1,0:T(1,128)S(1)} %get-tuple-element.121) | copy-start | bytes 3076
  1.7 23.9 %copy-start.4 = (f32[1,256]{1,0:T(1,128)}, f32[1,256]{1,0:T(1,128)S(1)}, u32[]{:S(2)}) copy-start(f32[1,256]{1,0:T(1,128)S(1)} %get-tuple-element.119) | copy-start | bytes 3076
  1.7 23.9 %copy-start.10 = (f32[1,256]{1,0:T(1,128)}, f32[1,256]{1,0:T(1,128)S(1)}, u32[]{:S(2)}) copy-start(f32[1,256]{1,0:T(1,128)S(1)} %get-tuple-element.109) | copy-start | bytes 3076
  2.8 22.8 %copy-start.6 = (f32[1,256]{1,0:T(1,128)}, f32[1,256]{1,0:T(1,128)S(1)}, u32[]{:S(2)}) copy-start(f32[1,256]{1,0:T(1,128)S(1)} %get-tuple-element.108) | copy-start | bytes 3076
  3.8 21.8 %copy-start.8 = (f32[1,256]{1,0:T(1,128)}, f32[1,256]{1,0:T(1,128)S(1)}, u32[]{:S(2)}) copy-start(f32[1,256]{1,0:T(1,128)S(1)} %get-tuple-element.123) | copy-start | bytes 3076
  8.4 108.4 %all-to-all-start = ((bf16[128,2,256]{2,1,0:T(2,128)(2,1)}), bf16[128,2,256]{2,1,0:T(2,128)(2,1)S(1)}, u32[]{:S(2)}, u32[]{:S(2)}) async-start(bf16[128,2,256]{2,1,0:T(2,128)(2,1)} %reshape.27182), calls=%async_computation | async-start | bytes 262144 | tf_op jit(solution)/shard_map/all_to_all | solution.py:88
  19.9 5.7 %copy-start.16 = (s32[128,128]{1,0:T(8,128)S(1)}, s32[128,128]{1,0:T(8,128)}, u32[]{:S(2)}) copy-start(s32[128,128]{1,0:T(8,128)} %param.18) | copy-start | bytes 196612
  25.7 90.6 %copy-start.15 = (s32[128,128]{1,0:T(8,128)S(1)}, s32[128,128]{1,0:T(8,128)}, u32[]{:S(2)}) copy-start(s32[128,128]{1,0:T(8,128)} %param.17) | copy-start | bytes 196612
  25.7 90.7 %copy-start.73 = (s32[128,1]{0,1:T(1,128)S(1)}, s32[128,1]{0,1:T(1,128)}, u32[]{:S(2)}) copy-start(s32[128,1]{0,1:T(1,128)} %param.22) | copy-start | bytes 1540
  25.7 91.1 %copy-start.1 = (f32[128,128]{1,0:T(8,128)S(1)}, f32[128,128]{1,0:T(8,128)}, u32[]{:S(2)}) copy-start(f32[128,128]{1,0:T(8,128)} %param.15) | copy-start | bytes 196612
  117.2 5.8 %copy-start.14 = (f32[128,128]{1,0:T(8,128)S(1)}, f32[128,128]{1,0:T(8,128)}, u32[]{:S(2)}) copy-start(f32[128,128]{1,0:T(8,128)} %param.16) | copy-start | bytes 196612
  117.3 5.9 %copy-start.74 = (f32[4,12]{1,0:T(4,128)S(1)}, f32[4,12]{1,0:T(4,128)}, u32[]{:S(2)}) copy-start(f32[4,12]{1,0:T(4,128)} %param.20) | copy-start | bytes 580
  140.7 11.4 %copy-start.2 = (f32[8,16,256]{2,1,0:T(8,128)S(1)}, f32[8,16,256]{2,1,0:T(8,128)}, u32[]{:S(2)}) copy-start(f32[8,16,256]{2,1,0:T(8,128)} %param.25) | copy-start | bytes 393220
  142.3 27.4 %all-to-all-start.1 = ((bf16[128,2,2048]{2,1,0:T(2,128)(2,1)}), bf16[128,2,2048]{2,1,0:T(2,128)(2,1)S(1)}, u32[]{:S(2)}, u32[]{:S(2)}) async-start(bf16[128,2,2048]{2,1,0:T(2,128)(2,1)} %reshape.27184), calls=%async_computation.1 | async-start | bytes 2097152 | tf_op jit(solution)/shard_map/all_to_all | solution.py:106
  (53 other events, 64.3 us)
